TPU v7x, 256 devices: a whole 4x4x8 slice. The times are simulated.
256 devices in a mesh: grp: 8 (over x, core), dev: 32 (over z, y).
Axes of the slice: x: 4, y: 4, z: 8, core: 2. Of those that a mesh axis runs over, the one named last changes fastest.
Arguments:
- references: bfloat16 [192, 2048], P('dev'), may hold values from -4 to 4
- particles: bfloat16 [2048, 65536], P(None, ('grp', 'dev')), may hold values from -1300 to 1300
- defocus_bin: int32 [65536], P(('grp', 'dev')), may hold values from 0 to 63
- contrast_table: float32 [64, 32], replicated, may hold values from 0.1 to 1
- noise_power: float32 [32], replicated, may hold values from 300 to 3000
- class_prior: float32 [192], replicated, may hold values from -3 to 3
Outputs:
- new_references: float32 [192, 2048], P('dev')
- occupancy: float32 [192], P('dev')
All inputs are finite; a program needn't handle non-finite values.
Results may differ from a plain program's by a relative error of at most 0.0015.
Values may be sent and summed in bfloat16 or wider, within the bound.
No kernel may reach another device: no remote copies, remote signals or barrier semaphores. Data moves between devices by JAX's collectives and lax.ppermute only.
A program may use at most 64 MiB of HBM per device.

v0:
```python
import math
import jax
import jax.numpy as jnp
from jax import lax
from jax.sharding import PartitionSpec as P

Q = 32
M = 32
R = 128
CLS_DEV = 6


def angle_tables(cycle_freqs, count_turns):
    freq_index = jnp.arange(cycle_freqs, dtype=jnp.int32)
    turn_index = jnp.arange(count_turns, dtype=jnp.int32)
    wrapped = freq_index[:, None] * turn_index[None, :] % count_turns
    phases = 2.0 * math.pi / count_turns * wrapped.astype(jnp.float32)
    factor = jnp.where(freq_index == 0, 1.0, 2.0).astype(jnp.float32)[:, None]
    cosine = jnp.cos(phases)
    sine_part = jnp.sin(phases)
    score_table = jnp.stack([factor * cosine, factor * sine_part], 0).astype(jnp.bfloat16)
    turn_table = jnp.stack([cosine, sine_part], 0).astype(jnp.bfloat16)
    return (score_table, turn_table)


def particle_terms(particles, defocus_bin, contrast_table, noise_power):
    columns = particles.shape[1]
    cycle_count = contrast_table.shape[1]
    freq_count = particles.shape[0] // (2 * cycle_count)
    onehot = (
        defocus_bin[None, :] == jnp.arange(contrast_table.shape[0], dtype=jnp.int32)[:, None]
    ).astype(jnp.float32)
    contrast = jnp.dot(contrast_table.T, onehot, precision=lax.Precision.HIGHEST)
    scaled = contrast / noise_power[:, None]
    power_term = contrast * scaled
    weighted = (
        particles.astype(jnp.float32).reshape(freq_count, 2, cycle_count, columns)
        * scaled[None, None]
    ).astype(jnp.bfloat16)
    return (weighted.reshape(freq_count, 2 * cycle_count, columns), power_term)


def class_rows(class_block):
    classes = class_block.shape[0]
    class_grid = class_block.reshape(classes, M, 2, Q)
    real_part = class_grid[:, :, 0, :]
    imag_part = class_grid[:, :, 1, :]
    rows_real = jnp.concatenate([real_part, imag_part], -1)
    rows_imag = jnp.concatenate([-imag_part, real_part], -1)
    stacked = jnp.stack([rows_real, rows_imag], 0)
    factor = jnp.where(jnp.arange(M) == 0, 1.0, 2.0).astype(jnp.float32)
    squares = class_grid.astype(jnp.float32) ** 2
    cycle_power = jnp.sum(jnp.sum(squares, axis=2) * factor[None, :, None], axis=1)
    return (stacked, cycle_power)


def block_rows(total_rows):
    return CLS_DEV * math.gcd(total_rows // CLS_DEV, 4)


def local(references, particles, defocus_bin, contrast_table, noise_power, class_prior):
    weighted, power_term = particle_terms(particles, defocus_bin, contrast_table, noise_power)
    score_table, turn_table = angle_tables(M, R)
    columns = particles.shape[1]
    classes_total = CLS_DEV * lax.axis_size("dev")

    def block_scores(class_block, first_row):
        stacked, cycle_power = class_rows(class_block)
        prior_part = lax.dynamic_slice_in_dim(class_prior, first_row, class_block.shape[0], 0)
        crossed = jnp.einsum(
            "pkmc,mcb->pmkb", stacked, weighted, preferred_element_type=jnp.float32
        ).astype(jnp.bfloat16)
        scores = jnp.einsum(
            "pmkb,pmr->krb", crossed, score_table, preferred_element_type=jnp.float32
        )
        penalty = jnp.dot(cycle_power, power_term, precision=lax.Precision.HIGHEST)
        return scores - 0.5 * penalty[:, None, :] + prior_part[:, None, None]

    initial = (jnp.full((columns,), -1e30, jnp.float32), jnp.zeros((columns,), jnp.float32))
    empty_sums = (
        jnp.zeros((classes_total, 2 * M * Q), jnp.float32),
        jnp.zeros((classes_total, Q), jnp.float32),
        jnp.zeros((classes_total,), jnp.float32),
    )
    gathered = lax.all_gather(references, "dev", axis=0, tiled=True)
    height = block_rows(gathered.shape[0])
    block_count = gathered.shape[0] // height
    blocks = gathered.reshape(block_count, height, gathered.shape[1])

    def one_block(current, block_item):
        class_block, offset = block_item
        scores = block_scores(class_block, offset * height)
        block_max = jnp.max(scores, axis=(0, 1))
        new_max = jnp.maximum(current[0], block_max)
        block_total = jnp.sum(jnp.exp(scores - new_max[None, None, :]), axis=(0, 1))
        return ((new_max, current[1] * jnp.exp(current[0] - new_max) + block_total), None)

    result, unused = lax.scan(
        one_block, initial, (blocks, jnp.arange(block_count, dtype=jnp.int32))
    )
    log_norm = result[0] + jnp.log(result[1])
    add_height = block_rows(gathered.shape[0])
    block_count = gathered.shape[0] // add_height
    blocks = gathered.reshape(block_count, add_height, gathered.shape[1])

    def one_block(current, block_item):
        class_block, offset = block_item
        row_start = offset * add_height
        scores = block_scores(class_block, row_start)
        responsibility = jnp.exp(scores - log_norm[None, None, :]).astype(jnp.bfloat16)
        spectra = jnp.einsum(
            "krb,pmr->pmkb", responsibility, turn_table, preferred_element_type=jnp.float32
        ).astype(jnp.bfloat16)
        products = jnp.einsum(
            "pmkb,mcb->kpmc", spectra, weighted, preferred_element_type=jnp.float32
        )
        real_sum = products[:, 0, :, :Q] + products[:, 1, :, Q:]
        imag_sum = products[:, 0, :, Q:] - products[:, 1, :, :Q]
        numerator = jnp.stack([real_sum, imag_sum], 2).reshape(add_height, 2 * M * Q)
        class_weight = jnp.sum(responsibility.astype(jnp.float32), axis=1)
        cycle_sum = jnp.dot(class_weight, power_term.T, precision=lax.Precision.HIGHEST)
        class_mass = jnp.sum(class_weight, axis=1)
        updated = (
            lax.dynamic_update_slice_in_dim(current[0], numerator, row_start, 0),
            lax.dynamic_update_slice_in_dim(current[1], cycle_sum, row_start, 0),
            lax.dynamic_update_slice_in_dim(current[2], class_mass, row_start, 0),
        )
        return (updated, None)

    result, unused = lax.scan(
        one_block, empty_sums, (blocks, jnp.arange(block_count, dtype=jnp.int32))
    )
    numer_all, cycles_all, mass_all = result
    width = numer_all.shape[1]
    packed = jnp.concatenate(
        [numer_all, cycles_all, mass_all[:, None], jnp.zeros((classes_total, 95), jnp.float32)], 1
    )
    packed = packed.reshape(lax.axis_size("dev"), CLS_DEV, packed.shape[1])
    own = lax.psum_scatter(packed, "dev", scatter_dimension=0, tiled=False)
    own = lax.psum(own, "grp")
    numerator = own[:, :width]
    cycle_sum = own[:, width : width + Q]
    class_mass = own[:, width + Q]
    new_references = (numerator.reshape(CLS_DEV, M, 2, Q) / cycle_sum[:, None, None, :]).reshape(
        CLS_DEV, 2 * M * Q
    )
    particle_total = columns * lax.axis_size("grp") * lax.axis_size("dev")
    occupancy = class_mass * (classes_total / particle_total)
    return (new_references, occupancy)


def solution(mesh):
    return jax.shard_map(
        local,
        mesh=mesh,
        in_specs=(P("dev", None), P(None, ("grp", "dev")), P(("grp", "dev")), P(), P(), P()),
        out_specs=(P("dev", None), P("dev")),
        check_vma=False,
    )
```

profile of v0, /device:TPU:8, one launch (start us, length us, event | category | flops | bytes accessed | tf_op | source)
XLA Modules:
  0.0 494.4 jit_solution(4730013904374642111)
XLA Ops:
  7.5 53.1 %all-gather = bf16[32,6,2048]{2,1,0:T(8,128)(2,1)S(1)} all-gather(bf16[1,6,2048]{2,1,0:T(8,128)(2,1)} %bitcast.182), channel_id=1, replica_groups=mesh['grp'=8,'dev'=32] {'dev'}, dimensions={0}, use_global_device_ids=true | all-gather | bytes 811008 | tf_op jit(solution)/shard_map/all_gather | solution.py:85
  62.6 1.2 fusion.39
  63.9 87.8 %while.28 = (s32[]{:T(128)}, f32[256]{0:T(256)S(1)}, f32[256]{0:T(256)S(1)}, bf16[8,24,2048]{2,1,0:T(8,128)(2,1)}, bf16[32,64,256]{2,1,0:T(8,128)(2,1)}, /*index...) while((s32[]{:T(128)}, f32[256]{0:T(256)S(1)}, ...), condition=%wide.region_5.6_spmd.clone, body=%wide.region_0.5_spmd.clone.sunk | while | flops 159947328 | bytes 10727242 | solution.py:98
  66.7 2.5 fusion.112
  71.9 2.0 fusion.113
  77.6 2.5 fusion.112
  82.9 2.0 fusion.113
  88.6 2.5 fusion.112
  93.9 2.0 fusion.113
  99.6 2.5 fusion.112
  104.9 2.0 fusion.113
  110.6 2.5 fusion.112
  115.8 2.0 fusion.113
  121.6 2.5 fusion.112
  126.8 2.0 fusion.113
  132.5 2.5 fusion.112
  137.8 2.0 fusion.113
  143.5 2.5 fusion.112
  148.8 2.0 fusion.113
  152.0 106.6 %while.27 = (s32[]{:T(128)}, f32[192,2048]{1,0:T(8,128)S(1)}, f32[192,32]{1,0:T(8,128)S(1)}, f32[192]{0:T(256)S(1)}, bf16[8,24,2048]{2,1,0:T(8,128)(2,1)}, /*ind...) while((s32[]{:T(128)}, f32[192,2048]{1,0:T(8,128)S(1)}, ...), condition=%wide.region_11.12_spmd, body=%wide.region_6.11_spmd.sunk | while | flops 313785664 | bytes 12832803 | solution.py:130
  154.9 1.6 fusion.102
  159.3 1.3 convert_reduce_fusion.3
  161.0 2.0 convolution_bitcast_fusion.3
  168.2 1.6 fusion.102
  172.6 1.3 convert_reduce_fusion.3
  174.3 2.0 convolution_bitcast_fusion.3
  181.5 1.6 fusion.102
  185.9 1.3 convert_reduce_fusion.3
  187.6 2.0 convolution_bitcast_fusion.3
  194.8 1.6 fusion.102
  199.2 1.3 convert_reduce_fusion.3
  200.9 2.0 convolution_bitcast_fusion.3
  208.1 1.6 fusion.102
  212.5 1.3 convert_reduce_fusion.3
  214.2 2.0 convolution_bitcast_fusion.3
  221.4 1.6 fusion.102
  225.8 1.3 convert_reduce_fusion.3
  227.5 2.0 convolution_bitcast_fusion.3
  234.7 1.6 fusion.102
  239.1 1.3 convert_reduce_fusion.3
  240.8 2.0 convolution_bitcast_fusion.3
  248.0 1.6 fusion.102
  252.4 1.3 convert_reduce_fusion.3
  254.1 2.0 convolution_bitcast_fusion.3
  259.7 1.5 concatenate.22
  261.4 2.2 concatenate.25
  263.6 197.4 %reduce-scatter.4.cloned.1.call-done = f32[1,6,2176]{2,1,0:T(8,128)} async-done(((f32[32,6,2176]{2,1,0:T(8,128)}), f32[1,6,2176]{2,1,0:T(8,128)}) %reduce-scatter.4.cloned.1.call-update) | async-done | bytes 52240
  461.0 24.9 %psum.7 = f32[6,2176]{1,0:T(8,128)S(1)} all-reduce(f32[6,2176]{1,0:T(8,128)} %bitcast.181), channel_id=1, replica_groups=mesh['grp'=8,'dev'=32] {'grp'}, use_global_device_ids=true, to_apply=%region_13.14 | all-reduce | flops 13056 | bytes 104448 | tf_op jit(solution)/shard_map/psum | solution.py:140
  (330 shorter events, 113.1 us)
Async XLA Ops:
  7.2 54.6 %copy-start = (f32[64,32]{0,1:T(8,128)S(1)}, f32[64,32]{0,1:T(8,128)}, u32[]{:S(2)}) copy-start(f32[64,32]{0,1:T(8,128)} %param.13) | copy-start | bytes 24580
  7.2 55.5 %copy-start.2 = (bf16[2048,256]{1,0:T(8,128)(2,1)S(1)}, bf16[2048,256]{1,0:T(8,128)(2,1)}, u32[]{:S(2)}) copy-start(bf16[2048,256]{1,0:T(8,128)(2,1)} %param.11) | copy-start | bytes 3145732
  7.2 56.7 %copy-start.3 = (f32[192]{0:T(256)S(1)}, f32[192]{0:T(256)}, u32[]{:S(2)}) copy-start(f32[192]{0:T(256)} %param.15) | copy-start | bytes 2308
  7.2 453.8 %reduce-scatter.4.cloned.1.call-start = ((), (), s32[]{:S(2)}) async-start(), calls=%async_computation.1 | async-start | bytes 2297856
  258.5 1.2 copy-start.1
Sparse Core Ops, SparseCore 0:
  263.7 197.2 reduce-scatter.3
where the time goes:
time: 497 us; the launch traced here: 494 us
  waiting for transfers between devices  197 us (40%)
  matrix products  82.1 us (17%)
  blocking collectives  78 us (16%)
  local copies, waits for them, and re-layouts  68.5 us (14%)
  other arithmetic  42 us (8%)
  between operations  14.2 us (3%)
  loops' own time  12.1 us (2%)
    unnamed x2, waiting for transfers between devices  197 us
    all_gather x1, blocking collectives, local(): gathered = lax.all_gather(references, 'dev', axis=0, tiled=True)  53.1 us
    dot_general x16, matrix products, block_scores(): jnp.einsum('pkmc,mcb->pmkb', stacked, weighted, preferred_element_type=jn...  32.7 us
    dot_general x16, matrix products, block_scores(): jnp.einsum('pmkb,pmr->krb', crossed, score_table, preferred_element_type=...  26.3 us
    psum x1, blocking collectives, local(): own = lax.psum(own, 'grp')  24.9 us
    dynamic_slice x32, local copies, waits for them, and re-layouts, local(): lax.scan(one_block, initial, (blocks, jnp.arange(block_count, dtype=jnp.i...  23.9 us
    reduce_sum x16, other arithmetic, class_rows(): jnp.sum(squares, axis=2) * factor[None, :, None]  18.6 us
    dot_general x8, matrix products, one_block(): jnp.einsum('pmkb,mcb->kpmc', spectra, weighted, preferred_element_type=jn...  15.7 us
  transfers between devices with their start and end apart: 1, of which 1 were waited for; matrix products, arithmetic and copies ran while one was open for 0% of the time, Pallas kernels for 0%

commit v1 on v0

--- a/solution.py
+++ b/solution.py
@@ -82,7 +82,8 @@
         jnp.zeros((classes_total, Q), jnp.float32),
         jnp.zeros((classes_total,), jnp.float32),
     )
-    gathered = lax.all_gather(references, "dev", axis=0, tiled=True)
+    sent = jnp.stack([references] * lax.axis_size("dev"))
+    gathered = jnp.concatenate(lax.all_to_all(sent, "dev", 0, 0), axis=0)
     height = block_rows(gathered.shape[0])
     block_count = gathered.shape[0] // height
     blocks = gathered.reshape(block_count, height, gathered.shape[1])

time: 497 us -> 482 us (0.970)
  blocking collectives: 78 us -> 24.9 us
  waiting for transfers between devices: 197 us -> 223 us
  starting transfers between devices: 0.04 us -> 11.9 us
    all_gather x1 -> x0, blocking collectives: 53.1 us -> none  [local(): gathered = lax.all_gather(references, 'dev', axis=0, tiled=True)]
    all_to_all x0 -> x1, waiting for transfers between devices: none -> 26.3 us  [local(): gathered = jnp.concatenate(lax.all_to_all(sent, 'dev', 0, 0), axis=0)]
    all_to_all x0 -> x1, starting transfers between devices: none -> 11.8 us  [local(): gathered = jnp.concatenate(lax.all_to_all(sent, 'dev', 0, 0), axis=0)]
  transfers between devices with their start and end apart: 1 -> 2, of which waited for: 1 -> 2; matrix products, arithmetic and copies ran while one was open for 0% -> 0% of each run, Pallas kernels for 0% -> 0%
where the time goes in v1:
time: 482 us; the launch traced here: 480 us
  waiting for transfers between devices  223 us (46%)
  matrix products  81.4 us (17%)
  local copies, waits for them, and re-layouts  70.5 us (15%)
  other arithmetic  42 us (9%)
  blocking collectives  24.9 us (5%)
  between operations  14.3 us (3%)
  loops' own time  12.1 us (3%)
  starting transfers between devices  11.9 us (2%)
    unnamed x2, waiting for transfers between devices  196 us
    dot_general x16, matrix products, block_scores(): jnp.einsum('pkmc,mcb->pmkb', stacked, weighted, preferred_element_type=jn...  32.7 us
    all_to_all x1, waiting for transfers between devices, local(): gathered = jnp.concatenate(lax.all_to_all(sent, 'dev', 0, 0), axis=0)  26.3 us
    dot_general x16, matrix products, block_scores(): jnp.einsum('pmkb,pmr->krb', crossed, score_table, preferred_element_type=...  26.3 us
    psum x1, blocking collectives, local(): own = lax.psum(own, 'grp')  24.9 us
    dynamic_slice x32, local copies, waits for them, and re-layouts, local(): lax.scan(one_block, initial, (blocks, jnp.arange(block_count, dtype=jnp.i...  23.9 us
    reduce_sum x16, other arithmetic, class_rows(): jnp.sum(squares, axis=2) * factor[None, :, None]  18.6 us
    dot_general x8, matrix products, one_block(): jnp.einsum('pmkb,mcb->kpmc', spectra, weighted, preferred_element_type=jn...  15.7 us
  transfers between devices with their start and end apart: 2, of which 2 were waited for; matrix products, arithmetic and copies ran while one was open for 0% of the time, Pallas kernels for 0%

profile of v1, /device:TPU:8, one launch (start us, length us, event | category | flops | bytes accessed | tf_op | source)
XLA Modules:
  0.0 479.8 jit_solution(3250641396538998352)
XLA Ops:
  7.2 2.0 stack.22
  9.2 11.8 %all-to-all-start = ((bf16[32,6,2048]{2,1,0:T(8,128)(2,1)}), bf16[32,6,2048]{2,1,0:T(8,128)(2,1)S(1)}, u32[]{:S(2)}, u32[]{:S(2)}) async-start(bf16[32,6,2048]{2,1,0:T(8,128)(2,1)} %stack.22), calls=%async_computation | async-start | bytes 2097152 | tf_op jit(solution)/shard_map/all_to_all | solution.py:86
  22.8 26.3 %all-to-all-done = bf16[32,6,2048]{2,1,0:T(8,128)(2,1)S(1)} async-done(((bf16[32,6,2048]{2,1,0:T(8,128)(2,1)}), bf16[32,6,2048]{2,1,0:T(8,128)(2,1)S(1)}, u32[]{:S(2)}, u32[]{:S(2)}) %all-to-all-start) | async-done | bytes 786464 | tf_op jit(solution)/shard_map/all_to_all | solution.py:86
  50.3 87.8 %while.28 = (s32[]{:T(128)}, f32[256]{0:T(256)S(1)}, f32[256]{0:T(256)S(1)}, bf16[8,24,2048]{2,1,0:T(8,128)(2,1)}, bf16[32,64,256]{2,1,0:T(8,128)(2,1)}, /*index...) while((s32[]{:T(128)}, f32[256]{0:T(256)S(1)}, ...), condition=%wide.region_5.6_spmd.clone, body=%wide.region_0.5_spmd.clone.sunk | while | flops 159947328 | bytes 10727242 | solution.py:99
  53.1 2.5 fusion.112
  58.3 2.0 fusion.113
  64.1 2.5 fusion.112
  69.3 2.0 fusion.113
  75.0 2.5 fusion.112
  80.3 2.0 fusion.113
  86.0 2.5 fusion.112
  91.3 2.0 fusion.113
  97.0 2.5 fusion.112
  102.3 2.0 fusion.113
  108.0 2.5 fusion.112
  113.2 2.0 fusion.113
  119.0 2.5 fusion.112
  124.2 2.0 fusion.113
  129.9 2.5 fusion.112
  135.2 2.0 fusion.113
  138.4 106.6 %while.27 = (s32[]{:T(128)}, f32[192,2048]{1,0:T(8,128)S(1)}, f32[192,32]{1,0:T(8,128)S(1)}, f32[192]{0:T(256)S(1)}, bf16[8,24,2048]{2,1,0:T(8,128)(2,1)}, /*ind...) while((s32[]{:T(128)}, f32[192,2048]{1,0:T(8,128)S(1)}, ...), condition=%wide.region_11.12_spmd, body=%wide.region_6.11_spmd.sunk | while | flops 313785664 | bytes 12832803 | solution.py:131
  141.3 1.6 fusion.102
  147.4 2.0 convolution_bitcast_fusion.3
  154.6 1.6 fusion.102
  159.0 1.3 convert_reduce_fusion.3
  160.7 2.0 convolution_bitcast_fusion.3
  167.9 1.6 fusion.102
  172.3 1.3 convert_reduce_fusion.3
  174.0 2.0 convolution_bitcast_fusion.3
  181.2 1.6 fusion.102
  185.6 1.3 convert_reduce_fusion.3
  187.3 2.0 convolution_bitcast_fusion.3
  194.5 1.6 fusion.102
  198.9 1.3 convert_reduce_fusion.3
  200.6 2.0 convolution_bitcast_fusion.3
  207.8 1.6 fusion.102
  212.2 1.3 convert_reduce_fusion.3
  213.9 2.0 convolution_bitcast_fusion.3
  221.1 1.6 fusion.102
  225.5 1.3 convert_reduce_fusion.3
  227.2 2.0 convolution_bitcast_fusion.3
  234.4 1.6 fusion.102
  238.8 1.3 convert_reduce_fusion.3
  240.5 2.0 convolution_bitcast_fusion.3
  246.1 1.5 concatenate.22
  247.8 2.2 concatenate.25
  250.0 196.4 %reduce-scatter.4.cloned.1.call-done = f32[1,6,2176]{2,1,0:T(8,128)} async-done(((f32[32,6,2176]{2,1,0:T(8,128)}), f32[1,6,2176]{2,1,0:T(8,128)}) %reduce-scatter.4.cloned.1.call-update) | async-done | bytes 52240
  446.5 24.9 %psum.7 = f32[6,2176]{1,0:T(8,128)S(1)} all-reduce(f32[6,2176]{1,0:T(8,128)} %bitcast.180), channel_id=1, replica_groups=mesh['grp'=8,'dev'=32] {'grp'}, use_global_device_ids=true, to_apply=%region_13.14 | all-reduce | flops 13056 | bytes 104448 | tf_op jit(solution)/shard_map/psum | solution.py:141
  (336 shorter events, 115.0 us)
Async XLA Ops:
  7.2 14.2 %copy-start = (f32[64,32]{0,1:T(8,128)S(1)}, f32[64,32]{0,1:T(8,128)}, u32[]{:S(2)}) copy-start(f32[64,32]{0,1:T(8,128)} %param.13) | copy-start | bytes 24580
  7.2 14.2 %copy-start.3 = (s32[256]{0:T(256)S(1)}, s32[256]{0:T(256)}, u32[]{:S(2)}) copy-start(s32[256]{0:T(256)} %param.12) | copy-start | bytes 3076
  7.2 14.2 %copy-start.5 = (f32[32]{0:T(128)S(1)}, f32[32]{0:T(128)}, u32[]{:S(2)}) copy-start(f32[32]{0:T(128)} %param.14) | copy-start | bytes 388
  7.2 14.3 %copy-start.2 = (bf16[2048,256]{1,0:T(8,128)(2,1)S(1)}, bf16[2048,256]{1,0:T(8,128)(2,1)}, u32[]{:S(2)}) copy-start(bf16[2048,256]{1,0:T(8,128)(2,1)} %param.11) | copy-start | bytes 3145732
  9.2 41.1 %copy-start.4 = (f32[192]{0:T(256)S(1)}, f32[192]{0:T(256)}, u32[]{:S(2)}) copy-start(f32[192]{0:T(256)} %param.15) | copy-start | bytes 2308
  9.2 39.9 %all-to-all-start = ((bf16[32,6,2048]{2,1,0:T(8,128)(2,1)}), bf16[32,6,2048]{2,1,0:T(8,128)(2,1)S(1)}, u32[]{:S(2)}, u32[]{:S(2)}) async-start(bf16[32,6,2048]{2,1,0:T(8,128)(2,1)} %stack.22), calls=%async_computation | async-start | bytes 2097152 | tf_op jit(solution)/shard_map/all_to_all | solution.py:86
  21.1 425.4 %reduce-scatter.4.cloned.1.call-start = ((), (), s32[]{:S(2)}) async-start(), calls=%async_computation.2 | async-start | bytes 2297856
  244.9 1.2 copy-start.1
Sparse Core Ops, SparseCore 0:
  250.1 196.2 reduce-scatter.3
